TPU v7x, 32 devices: a whole 2x2x4 slice. The times are simulated.
32 devices in a mesh: tm: 4 (over y, x), chan: 8 (over z, core).
Axes of the slice: x: 2, y: 2, z: 4, core: 2. Of those that a mesh axis runs over, the one named last changes fastest.
Arguments:
- strain: bfloat16 [256, 16384], P('chan', 'tm'), may hold values from -6 to 6
- fir_taps: bfloat16 [256, 256], P('chan'), may hold values from -0.375 to 0.375
Outputs:
- stacked: float32 [2, 256, 256, 256], P(None, 'tm', 'chan')
All inputs are finite; a program needn't handle non-finite values.
Results may differ from a plain program's by a relative error of at most 0.0062.
Values may be sent and summed in bfloat16 or wider, within the bound.
No kernel may reach another device: no remote copies, remote signals or barrier semaphores. Data moves between devices by JAX's collectives and lax.ppermute only.
A program may use at most 128 MiB of HBM per device.

v0:
```python
import math
import jax
import jax.numpy as jnp
from jax import lax
from jax.sharding import PartitionSpec as P

SEG = 512


def shifted(value, axis, by):
    size = lax.axis_size(axis)
    pairs = [(i, i + by) for i in range(size) if 0 <= i + by < size]
    return lax.ppermute(value, axis, pairs)


def make_table():
    sample_idx = jnp.arange(SEG, dtype=jnp.int32)
    bin_idx = jnp.arange(SEG // 2, dtype=jnp.int32)
    phases = sample_idx[:, None] * bin_idx[None, :] % SEG
    angles = phases.astype(jnp.float32) * (2.0 * math.pi / SEG)
    window = 0.5 - 0.5 * jnp.cos(sample_idx.astype(jnp.float32) * (2.0 * math.pi / SEG))
    cosine = window[:, None] * jnp.cos(angles)
    sine_part = -window[:, None] * jnp.sin(angles)
    return jnp.stack([cosine, sine_part], axis=1).astype(jnp.bfloat16)


def toeplitz(fir_taps):
    tap_count = fir_taps.shape[1]
    row_idx = jnp.arange(2 * tap_count, dtype=jnp.int32)[:, None]
    col_idx = jnp.arange(tap_count, dtype=jnp.int32)[None, :]
    lag_idx = col_idx + tap_count - row_idx
    valid = (lag_idx >= 0) & (lag_idx < tap_count)
    picked = jnp.take(fir_taps, jnp.clip(lag_idx, 0, tap_count - 1), axis=1)
    return jnp.where(valid[None, :, :], picked, jnp.zeros_like(picked))


def cross_block(own_bins, other_bins):
    swapped = jnp.stack([-other_bins[:, 1], other_bins[:, 0]], axis=1)
    real_part = jnp.einsum(
        "kpsi,kpsj->kij", own_bins, other_bins, preferred_element_type=jnp.float32
    )
    imag_part = jnp.einsum("kpsi,kpsj->kij", own_bins, swapped, preferred_element_type=jnp.float32)
    return jnp.stack([real_part, imag_part], axis=0)


def shards(strain, fir_taps):
    tap_count = fir_taps.shape[1]
    channels = strain.shape[0]
    previous = shifted(strain[:, -tap_count:], "tm", 1)
    extended = jnp.concatenate([previous, strain], axis=1)[:, 1:]
    filtered = lax.conv_general_dilated(
        extended[None],
        jnp.flip(fir_taps, axis=1)[:, None, :],
        window_strides=(1,),
        padding="VALID",
        dimension_numbers=("NCH", "OIH", "NCH"),
        feature_group_count=channels,
        preferred_element_type=jnp.float32,
    )[0]
    whitened = filtered.reshape(channels, -1).astype(jnp.bfloat16)
    segments = whitened.reshape(channels, whitened.shape[1] // SEG, SEG)
    spectra = jnp.einsum(
        "csn,npk->kpsc", segments, make_table(), preferred_element_type=jnp.float32
    ).astype(jnp.bfloat16)
    gathered = lax.all_gather(spectra, "chan", axis=3, tiled=True)
    all_bins = lax.all_to_all(gathered, "tm", split_axis=0, concat_axis=2, tiled=True)
    factor = 1.0 / (all_bins.shape[2] * SEG)
    first_col = lax.axis_index("chan") * channels
    own_bins = lax.dynamic_slice_in_dim(all_bins, first_col, channels, 3)
    result = cross_block(own_bins, all_bins) * factor
    return result


def solution(mesh):
    placed = (P("chan", "tm"), P("chan", None))
    return jax.shard_map(
        shards, mesh=mesh, in_specs=placed, out_specs=P(None, "tm", "chan", None), check_vma=False
    )
```

profile of v0, /device:TPU:0, one launch (start us, length us, event | category | flops | bytes accessed | tf_op | source)
XLA Modules:
  0.0 157.0 jit_solution(7761917013179768277)
XLA Ops:
  6.5 0.0 all-gather.2.cloned.1.call-start
  6.5 0.7 slice.12
  7.3 4.8 %collective-permute-start = (bf16[32,256]{1,0:T(8,128)(2,1)S(1)}, bf16[32,256]{1,0:T(8,128)(2,1)S(1)}, u32[]{:S(2)}, u32[]{:S(2)}) collective-permute-start(bf16[32,256]{1,0:T(8,128)(2,1)S(1)} %slice.12), channel_id=1, source_target_pairs={{0,8},{8,16},{16,24},{1,9},{9,17},{17,25},{2,10},{10,18},{18,26},{... | collective-permute-start | bytes 49160 | tf_op jit(solution)/shard_map/ppermute | solution.py:13
  12.2 2.3 %multiply_convert_fusion = (bf16[512,1,256]{2,0,1:T(8,128)(2,1)S(1)}, bf16[512,1,256]{2,0,1:T(8,128)(2,1)S(1)}) fusion(f32[512]{0:T(512)S(1)} %fusion.30, f32[512]{0:T(512)S(1)} %multiply_subtract_fusion), kind=kLoop, calls=%fused_computation.32 | loop fusion | flops 2359296 | bytes 528384 | tf_op jit(solution)/shard_map/convert.1
  14.5 0.9 rev.4
  15.4 0.1 copy.37
  15.5 0.0 collective-permute-done
  15.5 1.1 fusion.27
  16.6 0.6 reshape.125
  17.2 0.9 copy.36
  18.1 0.1 slice.18
  18.2 0.4 fusion.43
  18.6 0.0 copy-start
  18.6 61.0 %fusion.7 = bf16[8,544,32]{2,0,1:T(8,128)(2,1)S(1)} fusion(bf16[32,1,256]{0,1,2:T(2,128)(2,1)S(1)} %copy.37, bf16[32,8,799]{0,1,2:T(8,128)(2,1)S(1)} %fusion.43), kind=kOutput, calls=%fused_computation.10 | convolution fusion | flops 71303168 | bytes 704000 | tf_op jit(solution)/shard_map/conv_general_dilated | solution.py:51
  79.6 0.8 copy.38
  80.4 0.0 copy-done
  80.4 0.1 select_convert_fusion
  80.5 0.1 copy.39
  80.6 0.3 reshape.129
  80.9 0.1 copy.50
  81.0 1.0 fusion.15
  82.0 0.0 all-gather.2.cloned.1.call-update
  82.0 29.6 %all-gather.2.cloned.1.call-done = bf16[256,2,8,256]{0,3,2,1:T(8,128)(2,1)} async-done(((bf16[256,2,8,32]{0,3,2,1:T(8,128)(2,1)}), bf16[256,2,8,256]{0,3,2,1:T(8,128)(2,1)}) %all-gather.2.cloned.1.call-update) | async-done | bytes 2097168 | tf_op jit(solution)/shard_map/all_gather | solution.py:65
  111.6 4.5 %copy.41 = bf16[256,2,8,256]{3,2,1,0:T(8,128)(2,1)} copy(bf16[256,2,8,256]{0,3,2,1:T(8,128)(2,1)} %all-gather.2.cloned.1.call-done) | data formatting | bytes 4194304 | tf_op jit(solution)/shard_map/all_gather | solution.py:65
  116.1 3.6 %all-to-all-start = ((bf16[256,2,8,256]{3,2,1,0:T(8,128)(2,1)}), bf16[256,2,8,256]{3,2,1,0:T(8,128)(2,1)S(1)}, u32[]{:S(2)}, u32[]{:S(2)}) async-start(bf16[256,2,8,256]{3,2,1,0:T(8,128)(2,1)} %copy.41), calls=%async_computation | async-start | bytes 4194304 | tf_op jit(solution)/shard_map/all_to_all | solution.py:66
  119.7 25.5 %all-to-all-done = bf16[256,2,8,256]{3,2,1,0:T(8,128)(2,1)S(1)} async-done(((bf16[256,2,8,256]{3,2,1,0:T(8,128)(2,1)}), bf16[256,2,8,256]{3,2,1,0:T(8,128)(2,1)S(1)}, u32[]{:S(2)}, u32[]{:S(2)}) %all-to-all-start) | async-done | bytes 2097184 | tf_op jit(solution)/shard_map/all_to_all | solution.py:66
  145.2 0.3 copy.56
  145.5 0.1 slice_negate_fusion
  145.7 1.0 convolution_bitcast_fusion
  146.7 1.0 fusion.12
  147.7 2.5 %maximum_multiply_fusion = f32[2,64,32,256]{3,2,1,0:T(8,128)} fusion(f32[1,64,32,256]{3,2,1,0:T(8,128)S(1)} %fusion.12, f32[1,64,32,256]{3,2,1,0:T(8,128)S(1)} %convolution_bitcast_fusion), kind=kLoop, calls=%fused_computation | loop fusion | flops 2097152 | bytes 8388608 | tf_op jit(solution)/shard_map/mul | solution.py:70
  (4 shorter events, 0.1 us)
Async XLA Ops:
  6.5 105.1 %all-gather.2.cloned.1.call-start = ((), (), s32[]{:S(2)}) async-start(), calls=%async_computation.1 | async-start | bytes 2359296 | tf_op jit(solution)/shard_map/all_gather | solution.py:65
  7.3 8.3 %collective-permute-start = (bf16[32,256]{1,0:T(8,128)(2,1)S(1)}, bf16[32,256]{1,0:T(8,128)(2,1)S(1)}, u32[]{:S(2)}, u32[]{:S(2)}) collective-permute-start(bf16[32,256]{1,0:T(8,128)(2,1)S(1)} %slice.12), channel_id=1, source_target_pairs={{0,8},{8,16},{16,24},{1,9},{9,17},{17,25},{2,10},{10,18},{18,26},{... | collective-permute-start | bytes 49160 | tf_op jit(solution)/shard_map/ppermute | solution.py:13
  18.6 61.8 %copy-start = (pred[8,544]{1,0:T(8,128)(4,1)S(1)}, pred[8,544]{1,0:T(8,128)(4,1)}, u32[]{:S(2)}) copy-start(pred[8,544]{1,0:T(8,128)(4,1)} %constant.37) | copy-start | bytes 13060
  116.1 29.1 %all-to-all-start = ((bf16[256,2,8,256]{3,2,1,0:T(8,128)(2,1)}), bf16[256,2,8,256]{3,2,1,0:T(8,128)(2,1)S(1)}, u32[]{:S(2)}, u32[]{:S(2)}) async-start(bf16[256,2,8,256]{3,2,1,0:T(8,128)(2,1)} %copy.41), calls=%async_computation | async-start | bytes 4194304 | tf_op jit(solution)/shard_map/all_to_all | solution.py:66
Sparse Core Ops, SparseCore 0:
  82.1 29.4 all-gather.1
where the time goes:
time: 157 us
  matrix products  64.1 us (41%)
  waiting for transfers between devices  55.1 us (35%)
  between operations  13.6 us (9%)
  local copies, waits for them, and re-layouts  9.31 us (6%)
  starting transfers between devices  8.48 us (5%)
  other arithmetic  6.53 us (4%)
    conv_general_dilated x1, matrix products, shards(): lax.conv_general_dilated(extended[None], jnp.flip(fir_taps, axis=1)[:, No...  61 us
    all_gather x1, waiting for transfers between devices, shards(): gathered = lax.all_gather(spectra, 'chan', axis=3, tiled=True)  29.6 us
    all_to_all x1, waiting for transfers between devices, shards(): lax.all_to_all(gathered, 'tm', split_axis=0, concat_axis=2, tiled=True)  25.5 us
    ppermute x1, starting transfers between devices, shifted(): return lax.ppermute(value, axis, pairs)  4.83 us
    all_gather x1, local copies, waits for them, and re-layouts, shards(): gathered = lax.all_gather(spectra, 'chan', axis=3, tiled=True)  4.49 us
    all_to_all x1, starting transfers between devices, shards(): lax.all_to_all(gathered, 'tm', split_axis=0, concat_axis=2, tiled=True)  3.65 us
  transfers between devices with their start and end apart: 3, of which 2 were waited for; matrix products, arithmetic and copies ran while one was open for 2% of the time, Pallas kernels for 0%

commit v1 on v0

--- a/solution.py
+++ b/solution.py
@@ -5,6 +5,13 @@
 from jax.sharding import PartitionSpec as P
 
 SEG = 512
+
+
+def exchange_blocks(x, axis, split, join):
+    size = lax.axis_size(axis)
+    blocks = jnp.stack(jnp.split(x, size, axis=split), axis=0)
+    blocks = lax.all_to_all(blocks, axis, split_axis=0, concat_axis=0)
+    return jnp.concatenate(blocks, axis=join)
 
 
 def shifted(value, axis, by):
@@ -63,7 +70,7 @@
         "csn,npk->kpsc", segments, make_table(), preferred_element_type=jnp.float32
     ).astype(jnp.bfloat16)
     gathered = lax.all_gather(spectra, "chan", axis=3, tiled=True)
-    all_bins = lax.all_to_all(gathered, "tm", split_axis=0, concat_axis=2, tiled=True)
+    all_bins = exchange_blocks(gathered, "tm", 0, 2)
     factor = 1.0 / (all_bins.shape[2] * SEG)
     first_col = lax.axis_index("chan") * channels
     own_bins = lax.dynamic_slice_in_dim(all_bins, first_col, channels, 3)

time: 157 us -> 164 us (1.045)
  local copies, waits for them, and re-layouts: 9.31 us -> 13.5 us
  other arithmetic: 6.53 us -> 9.11 us
    another operation x0 -> x2, local copies, waits for them, and re-layouts: none -> 8.66 us  [exchange_blocks(): blocks = jnp.stack(jnp.split(x, size, axis=split), axis=0)]
    all_gather x1 -> x0, local copies, waits for them, and re-layouts: 4.49 us -> none  [shards(): gathered = lax.all_gather(spectra, 'chan', axis=3, tiled=True)]
    another operation x1 -> x2, other arithmetic: 2.31 us -> 4.9 us  [the longest x1 2.59 us: exchange_blocks(): blocks = jnp.stack(jnp.split(x, size, axis=split), axis=0)]
where the time goes in v1:
time: 164 us
  matrix products  64.1 us (39%)
  waiting for transfers between devices  55.1 us (34%)
  between operations  13.6 us (8%)
  local copies, waits for them, and re-layouts  13.5 us (8%)
  other arithmetic  9.11 us (6%)
  starting transfers between devices  8.48 us (5%)
    conv_general_dilated x1, matrix products, shards(): lax.conv_general_dilated(extended[None], jnp.flip(fir_taps, axis=1)[:, No...  61 us
    all_gather x1, waiting for transfers between devices, shards(): gathered = lax.all_gather(spectra, 'chan', axis=3, tiled=True)  29.6 us
    all_to_all x1, waiting for transfers between devices, exchange_blocks(): blocks = lax.all_to_all(blocks, axis, split_axis=0, concat_axis=0)  25.5 us
    another operation x2, local copies, waits for them, and re-layouts, exchange_blocks(): blocks = jnp.stack(jnp.split(x, size, axis=split), axis=0)  8.66 us
    ppermute x1, starting transfers between devices, shifted(): return lax.ppermute(value, axis, pairs)  4.83 us
    all_to_all x1, starting transfers between devices, exchange_blocks(): blocks = lax.all_to_all(blocks, axis, split_axis=0, concat_axis=0)  3.65 us
  transfers between devices with their start and end apart: 3, of which 2 were waited for; matrix products, arithmetic and copies ran while one was open for 2% of the time, Pallas kernels for 0%

profile of v1, /device:TPU:0, one launch (start us, length us, event | category | flops | bytes accessed | tf_op | source)
XLA Modules:
  0.0 163.8 jit_solution(16261302013762512850)
XLA Ops:
  6.5 0.0 all-gather.2.cloned.1.call-start
  6.5 0.7 slice.12
  7.3 4.8 %collective-permute-start = (bf16[32,256]{1,0:T(8,128)(2,1)S(1)}, bf16[32,256]{1,0:T(8,128)(2,1)S(1)}, u32[]{:S(2)}, u32[]{:S(2)}) collective-permute-start(bf16[32,256]{1,0:T(8,128)(2,1)S(1)} %slice.12), channel_id=1, source_target_pairs={{0,8},{8,16},{16,24},{1,9},{9,17},{17,25},{2,10},{10,18},{18,26},{... | collective-permute-start | bytes 49160 | tf_op jit(solution)/shard_map/ppermute | solution.py:20
  12.2 2.3 %multiply_convert_fusion = (bf16[512,1,256]{2,0,1:T(8,128)(2,1)S(1)}, bf16[512,1,256]{2,0,1:T(8,128)(2,1)S(1)}) fusion(f32[512]{0:T(512)S(1)} %fusion.30, f32[512]{0:T(512)S(1)} %multiply_subtract_fusion), kind=kLoop, calls=%fused_computation.37 | loop fusion | flops 2359296 | bytes 528384 | tf_op jit(solution)/shard_map/convert.1
  14.5 0.9 rev.4
  15.4 0.1 copy.32
  15.5 0.0 collective-permute-done
  15.5 1.1 fusion.27
  16.6 0.6 reshape.133
  17.2 0.9 copy.31
  18.1 0.1 slice.18
  18.2 0.4 fusion.43
  18.6 0.0 copy-start
  18.6 61.0 %fusion.7 = bf16[8,544,32]{2,0,1:T(8,128)(2,1)S(1)} fusion(bf16[32,1,256]{0,1,2:T(2,128)(2,1)S(1)} %copy.32, bf16[32,8,799]{0,1,2:T(8,128)(2,1)S(1)} %fusion.43), kind=kOutput, calls=%fused_computation.11 | convolution fusion | flops 71303168 | bytes 704000 | tf_op jit(solution)/shard_map/conv_general_dilated | solution.py:58
  79.6 0.8 copy.33
  80.4 0.0 copy-done
  80.4 0.1 select_convert_fusion
  80.5 0.1 copy.34
  80.6 0.3 reshape.137
  80.9 0.1 copy.43
  81.0 1.0 fusion.15
  82.0 0.0 all-gather.2.cloned.1.call-update
  82.0 29.6 %all-gather.2.cloned.1.call-done = bf16[256,2,8,256]{0,3,2,1:T(8,128)(2,1)} async-done(((bf16[256,2,8,32]{0,3,2,1:T(8,128)(2,1)}), bf16[256,2,8,256]{0,3,2,1:T(8,128)(2,1)}) %all-gather.2.cloned.1.call-update) | async-done | bytes 2097168 | tf_op jit(solution)/shard_map/all_gather | solution.py:72
  111.6 3.0 %slice_bitcast_fusion.3 = (bf16[1,64,2,8,256]{1,4,3,2,0:T(8,128)(2,1)S(1)}, bf16[1,64,2,8,256]{1,4,3,2,0:T(8,128)(2,1)S(1)}, bf16[1,64,2,8,256]{1,4,3,2,0:T(8,128)(2,1)S(1)}, bf16[1,64,2,8,256]{1,4,3,2,0:T(8,128)(2,1)S(1)}) fusion(bf16[256,2,8,256]{0,3,2,1:T(8,128)(2,1)} %all-gather.2.cloned.1.call-done), kind=kLoop, calls=%fused_computation.23 | loop fusion | bytes 4194304 | tf_op jit(solution)/shard_map/stack | solution.py:12
  114.6 2.6 %pad_maximum_fusion = bf16[4,64,2,8,256]{1,4,3,2,0:T(8,128)(2,1)} fusion(bf16[1,64,2,8,256]{1,4,3,2,0:T(8,128)(2,1)S(1)} %get-tuple-element.8, bf16[1,64,2,8,256]{1,4,3,2,0:T(8,128)(2,1)S(1)} %get-tuple-element.9, bf16[1,64,2,8,256]{1,4,3,2,0:T(8,128)(2,1)S(1)} %get-tuple-element.10, bf16[1,64,2,8,256]{1,4,3,2,0:T(8,128)(2,1)S(1)} %get-tuple-element.7), kind=kLoop, calls=%fused_computation | loop fusion | flops 3145728 | bytes 4194304 | tf_op jit(solution)/shard_map/stack | solution.py:12
  117.2 5.6 %copy.36 = bf16[4,64,2,8,256]{4,3,2,1,0:T(8,128)(2,1)} copy(bf16[4,64,2,8,256]{1,4,3,2,0:T(8,128)(2,1)} %pad_maximum_fusion) | data formatting | bytes 4194304 | tf_op jit(solution)/shard_map/stack | solution.py:12
  122.9 3.6 %all-to-all-start = ((bf16[4,64,2,8,256]{4,3,2,1,0:T(8,128)(2,1)}), bf16[4,64,2,8,256]{4,3,2,1,0:T(8,128)(2,1)S(1)}, u32[]{:S(2)}, u32[]{:S(2)}) async-start(bf16[4,64,2,8,256]{4,3,2,1,0:T(8,128)(2,1)} %copy.36), calls=%async_computation | async-start | bytes 4194304 | tf_op jit(solution)/shard_map/all_to_all | solution.py:13
  126.5 25.5 %all-to-all-done = bf16[4,64,2,8,256]{4,3,2,1,0:T(8,128)(2,1)S(1)} async-done(((bf16[4,64,2,8,256]{4,3,2,1,0:T(8,128)(2,1)}), bf16[4,64,2,8,256]{4,3,2,1,0:T(8,128)(2,1)S(1)}, u32[]{:S(2)}, u32[]{:S(2)}) %all-to-all-start) | async-done | bytes 2097184 | tf_op jit(solution)/shard_map/all_to_all | solution.py:13
  152.0 0.3 copy.49
  152.3 0.1 slice_negate_fusion
  152.4 1.0 convolution_bitcast_fusion
  153.4 1.0 fusion.12
  154.5 2.5 %maximum_multiply_fusion = f32[2,64,32,256]{3,2,1,0:T(8,128)} fusion(f32[1,64,32,256]{3,2,1,0:T(8,128)S(1)} %fusion.12, f32[1,64,32,256]{3,2,1,0:T(8,128)S(1)} %convolution_bitcast_fusion), kind=kLoop, calls=%fused_computation.1 | loop fusion | flops 2097152 | bytes 8388608 | tf_op jit(solution)/shard_map/mul | solution.py:77
  (4 shorter events, 0.1 us)
Async XLA Ops:
  6.5 105.1 %all-gather.2.cloned.1.call-start = ((), (), s32[]{:S(2)}) async-start(), calls=%async_computation.1 | async-start | bytes 2359296 | tf_op jit(solution)/shard_map/all_gather | solution.py:72
  7.3 8.3 %collective-permute-start = (bf16[32,256]{1,0:T(8,128)(2,1)S(1)}, bf16[32,256]{1,0:T(8,128)(2,1)S(1)}, u32[]{:S(2)}, u32[]{:S(2)}) collective-permute-start(bf16[32,256]{1,0:T(8,128)(2,1)S(1)} %slice.12), channel_id=1, source_target_pairs={{0,8},{8,16},{16,24},{1,9},{9,17},{17,25},{2,10},{10,18},{18,26},{... | collective-permute-start | bytes 49160 | tf_op jit(solution)/shard_map/ppermute | solution.py:20
  18.6 61.8 %copy-start = (pred[8,544]{1,0:T(8,128)(4,1)S(1)}, pred[8,544]{1,0:T(8,128)(4,1)}, u32[]{:S(2)}) copy-start(pred[8,544]{1,0:T(8,128)(4,1)} %constant.37) | copy-start | bytes 13060
  122.9 29.1 %all-to-all-start = ((bf16[4,64,2,8,256]{4,3,2,1,0:T(8,128)(2,1)}), bf16[4,64,2,8,256]{4,3,2,1,0:T(8,128)(2,1)S(1)}, u32[]{:S(2)}, u32[]{:S(2)}) async-start(bf16[4,64,2,8,256]{4,3,2,1,0:T(8,128)(2,1)} %copy.36), calls=%async_computation | async-start | bytes 4194304 | tf_op jit(solution)/shard_map/all_to_all | solution.py:13
Sparse Core Ops, SparseCore 0:
  82.1 29.4 all-gather.1
